TPU v7x, 256 devices: a whole 4x4x8 slice. The times are simulated.
256 devices in a mesh: prow: 64 (over x, z, core), pcol: 4 (over y).
Axes of the slice: x: 4, y: 4, z: 8, core: 2. Of those that a mesh axis runs over, the one named last changes fastest.
Arguments:
- right_side: float32 [512, 65536], P('pcol', 'prow'), may hold values from -6 to 6
- factor: float32 [65536, 2048], P('prow', 'pcol'), may hold values from -0.125 to 0.125
- inverses: float32 [2048, 512], replicated, as said below
Outputs:
- solved: float32 [512, 65536], P('pcol', 'prow')
Inputs may be any that keep to these rules, and one draw needn't show every extreme that they name: Each 512 x 512 block of inverses is lower triangular with a positive diagonal.
All inputs are finite; a program needn't handle non-finite values.
Results may differ from a plain program's by a relative error of at most 0.0001.
Values sent between devices are 32-bit elements; how exact they have to be, the bound alone decides.
No kernel may reach another device: no remote copies, remote signals or barrier semaphores. Data moves between devices by JAX's collectives and lax.ppermute only.
A program may use at most 64 MiB of HBM per device.

v0:
```python
import jax
import jax.numpy as jnp
from jax import lax
from jax.sharding import PartitionSpec as P


def spread(block, axis, source):
    block = jnp.where(lax.axis_index(axis) == source, block, jnp.zeros_like(block))
    return lax.psum(block, axis)


def contract(left, right):
    return lax.dot_general(
        left,
        right,
        (((1,), (1,)), ((), ())),
        precision=lax.Precision.HIGHEST,
        preferred_element_type=jnp.float32,
    )


def per_device(right_side, factor, inverses):
    block = factor.shape[1]
    rhs_width = right_side.shape[0]
    sections = lax.axis_size("pcol")
    all_samples = rhs_width * sections
    row_at = lax.axis_index("prow")
    col_at = lax.axis_index("pcol")
    top_block = factor[:block]
    panel_own = jnp.zeros((all_samples, block), jnp.float32)
    solved_head = jnp.zeros((rhs_width, block), jnp.float32)
    own_panels = []
    for section in range(sections):
        current = right_side[:, :block]
        if section > 0:
            current = current - lax.psum_scatter(
                contract(panel_own, top_block), "pcol", scatter_dimension=0, tiled=True
            )
        block_inverse = inverses[section * block : (section + 1) * block]
        solved_part = contract(current, block_inverse)
        solved_head = jnp.where(row_at == section, solved_part, solved_head)
        gathered = lax.all_gather(solved_part, "pcol", axis=0, tiled=True)
        panel_full = spread(gathered, "prow", section)
        panel_own = jnp.where(col_at == section, panel_full, panel_own)
        own_panels.append(lax.dynamic_slice_in_dim(panel_full, col_at * rhs_width, rhs_width, 0))
    updated = right_side - lax.psum_scatter(
        contract(panel_own, factor), "pcol", scatter_dimension=0, tiled=True
    )
    head_block = jnp.where(row_at < sections, solved_head, updated[:, :block])
    return jnp.concatenate([head_block, updated[:, block:]], axis=1)


def solution(mesh):
    return jax.shard_map(
        per_device,
        mesh=mesh,
        in_specs=(P("pcol", "prow"), P("prow", "pcol"), P()),
        out_specs=P("pcol", "prow"),
        check_vma=False,
    )
```

profile of v0, /device:TPU:1, one launch (start us, length us, event | category | flops | bytes accessed | tf_op | source)
XLA Modules:
  0.0 1011.9 jit_solution(13477425533814743867)
XLA Ops:
  6.5 0.0 all-gather.5.cloned.1.call-start
  6.5 3.2 fusion.8
  9.7 0.0 copy-start
  9.7 0.0 all-gather.5.cloned.1.call-update
  9.7 0.0 all-reduce.5.cloned.1.call-start
  9.8 29.5 %all-gather.5.cloned.1.call-done = f32[512,512]{1,0:T(8,128)} async-done(((f32[128,512]{1,0:T(8,128)}), f32[512,512]{1,0:T(8,128)}) %all-gather.5.cloned.1.call-update) | async-done | bytes 1048592 | tf_op jit(solution)/shard_map/all_gather | solution.py:42
  39.3 1.1 broadcast_select_fusion.3
  40.4 0.0 all-reduce.5.cloned.1.call-update
  40.4 0.0 reduce-scatter.5.cloned.1.call-start
  40.5 0.0 copy-start.1
  40.5 187.1 %all-reduce.5.cloned.1.call-done = f32[512,512]{1,0:T(8,128)} async-done(((f32[512,512]{1,0:T(8,128)}), f32[512,512]{1,0:T(8,128)}) %all-reduce.5.cloned.1.call-update) | async-done | bytes 1048592 | tf_op jit(solution)/shard_map/psum | solution.py:9
  227.6 0.0 copy-done
  227.6 4.1 fusion.10
  231.7 0.0 reduce-scatter.5.cloned.1.call-update
  231.7 0.0 all-gather.7.cloned.1.call-start
  231.8 22.7 %reduce-scatter.5.cloned.1.call-done = f32[128,512]{1,0:T(8,128)} async-done(((f32[512,512]{1,0:T(8,128)}), f32[128,512]{1,0:T(8,128)}) %reduce-scatter.5.cloned.1.call-update) | async-done | bytes 262160 | tf_op jit(solution)/shard_map/reduce_scatter | solution.py:36
  254.5 0.0 copy-done.1
  254.5 3.2 fusion.6
  257.7 0.0 all-gather.7.cloned.1.call-update
  257.7 0.0 all-reduce.7.cloned.1.call-start
  257.8 26.9 %all-gather.7.cloned.1.call-done = f32[512,512]{1,0:T(8,128)} async-done(((f32[128,512]{1,0:T(8,128)}), f32[512,512]{1,0:T(8,128)}) %all-gather.7.cloned.1.call-update) | async-done | bytes 1048592 | tf_op jit(solution)/shard_map/all_gather | solution.py:42
  284.6 2.3 broadcast_select_fusion.2
  286.9 0.0 all-reduce.7.cloned.1.call-update
  286.9 0.0 reduce-scatter.7.cloned.1.call-start
  287.0 185.8 %all-reduce.7.cloned.1.call-done = f32[512,512]{1,0:T(8,128)} async-done(((f32[512,512]{1,0:T(8,128)}), f32[512,512]{1,0:T(8,128)}) %all-reduce.7.cloned.1.call-update) | async-done | bytes 1048592 | tf_op jit(solution)/shard_map/psum | solution.py:9
  472.8 1.4 select_select_fusion
  474.2 2.8 fusion.14
  477.1 0.0 reduce-scatter.7.cloned.1.call-update
  477.1 0.0 all-gather.9.cloned.1.call-start
  477.1 22.7 %reduce-scatter.7.cloned.1.call-done = f32[128,512]{1,0:T(8,128)} async-done(((f32[512,512]{1,0:T(8,128)}), f32[128,512]{1,0:T(8,128)}) %reduce-scatter.7.cloned.1.call-update) | async-done | bytes 262160 | tf_op jit(solution)/shard_map/reduce_scatter | solution.py:36
  499.9 3.3 fusion.4
  503.1 0.0 all-gather.9.cloned.1.call-update
  503.2 0.0 all-reduce.9.cloned.1.call-start
  503.2 26.9 %all-gather.9.cloned.1.call-done = f32[512,512]{1,0:T(8,128)} async-done(((f32[128,512]{1,0:T(8,128)}), f32[512,512]{1,0:T(8,128)}) %all-gather.9.cloned.1.call-update) | async-done | bytes 1048592 | tf_op jit(solution)/shard_map/all_gather | solution.py:42
  530.2 1.1 broadcast_select_fusion.1
  531.2 0.0 all-reduce.9.cloned.1.call-update
  531.3 0.0 reduce-scatter.9.cloned.1.call-start
  531.3 187.1 %all-reduce.9.cloned.1.call-done = f32[512,512]{1,0:T(8,128)} async-done(((f32[512,512]{1,0:T(8,128)}), f32[512,512]{1,0:T(8,128)}) %all-reduce.9.cloned.1.call-update) | async-done | bytes 1048592 | tf_op jit(solution)/shard_map/psum | solution.py:9
  718.4 2.8 fusion.12
  721.3 0.0 reduce-scatter.9.cloned.1.call-update
  721.3 0.0 all-gather.11.cloned.1.call-start
  721.4 25.3 %reduce-scatter.9.cloned.1.call-done = f32[128,512]{1,0:T(8,128)} async-done(((f32[512,512]{1,0:T(8,128)}), f32[128,512]{1,0:T(8,128)}) %reduce-scatter.9.cloned.1.call-update) | async-done | bytes 262160 | tf_op jit(solution)/shard_map/reduce_scatter | solution.py:36
  746.6 3.3 fusion.2
  749.9 0.0 all-gather.11.cloned.1.call-update
  749.9 0.0 all-reduce.11.cloned.1.call-start
  750.0 26.9 %all-gather.11.cloned.1.call-done = f32[512,512]{1,0:T(8,128)} async-done(((f32[128,512]{1,0:T(8,128)}), f32[512,512]{1,0:T(8,128)}) %all-gather.11.cloned.1.call-update) | async-done | bytes 1048592 | tf_op jit(solution)/shard_map/all_gather | solution.py:42
  776.8 1.1 broadcast_select_fusion
  777.9 0.0 all-reduce.11.cloned.1.call-update
  777.9 0.2 reduce-scatter.11.cloned.1.call-start
  778.2 186.9 %all-reduce.11.cloned.1.call-done = f32[512,512]{1,0:T(8,128)} async-done(((f32[512,512]{1,0:T(8,128)}), f32[512,512]{1,0:T(8,128)}) %all-reduce.11.cloned.1.call-update) | async-done | bytes 1048592 | tf_op jit(solution)/shard_map/psum | solution.py:9
  965.1 4.9 fusion
  970.0 0.0 copy-start.2
  970.0 0.0 copy-start.6
  970.0 0.0 reduce-scatter.11.cloned.1.call-update
  970.1 32.8 %reduce-scatter.11.cloned.1.call-done = f32[128,1024]{1,0:T(8,128)} async-done(((f32[512,1024]{1,0:T(8,128)}), f32[128,1024]{1,0:T(8,128)}) %reduce-scatter.11.cloned.1.call-update) | async-done | bytes 524304 | tf_op jit(solution)/shard_map/reduce_scatter | solution.py:46
  1002.9 0.0 copy-done.2
  1002.9 1.1 sub.15
  1004.0 0.0 copy-done.3
  1004.0 0.0 copy-done.4
  1004.0 0.0 copy-done.5
  1004.1 0.0 copy-done.6
  1004.1 0.2 slice_select_fusion
  1004.2 0.0 copy-start.7
  1004.2 0.8 copy-done.7
  (4 shorter events, 0.0 us)
Async XLA Ops:
  6.5 32.8 %all-gather.5.cloned.1.call-start = ((), (), s32[]{:S(2)}) async-start(), calls=%async_computation.4 | async-start | bytes 1310720 | tf_op jit(solution)/shard_map/all_gather | solution.py:42
  9.7 217.9 %copy-start = (f32[1024,512]{1,0:T(8,128)S(1)}, f32[1024,512]{1,0:T(8,128)}, u32[]{:S(2)}) copy-start(f32[1024,512]{1,0:T(8,128)} %param.4) | copy-start | bytes 6291460
  9.7 217.9 %all-reduce.5.cloned.1.call-start = ((), (), s32[]{:S(2)}) async-start(), calls=%async_computation.5 | async-start | bytes 2097152 | tf_op jit(solution)/shard_map/psum | solution.py:9
  40.4 214.1 %reduce-scatter.5.cloned.1.call-start = ((), (), s32[]{:S(2)}) async-start(), calls=%async_computation.6 | async-start | bytes 1310720 | tf_op jit(solution)/shard_map/reduce_scatter | solution.py:36
  40.5 214.0 %copy-start.1 = (f32[128,1024]{1,0:T(8,128)S(1)}, f32[128,1024]{1,0:T(8,128)}, u32[]{:S(2)}) copy-start(f32[128,1024]{1,0:T(8,128)} %param.3) | copy-start | bytes 1572868
  231.7 52.9 %all-gather.7.cloned.1.call-start = ((), (), s32[]{:S(2)}) async-start(), calls=%async_computation.7 | async-start | bytes 1310720 | tf_op jit(solution)/shard_map/all_gather | solution.py:42
  257.7 215.0 %all-reduce.7.cloned.1.call-start = ((), (), s32[]{:S(2)}) async-start(), calls=%async_computation.8 | async-start | bytes 2097152 | tf_op jit(solution)/shard_map/psum | solution.py:9
  286.9 212.9 %reduce-scatter.7.cloned.1.call-start = ((), (), s32[]{:S(2)}) async-start(), calls=%async_computation.9 | async-start | bytes 1310720 | tf_op jit(solution)/shard_map/reduce_scatter | solution.py:36
  477.1 53.1 %all-gather.9.cloned.1.call-start = ((), (), s32[]{:S(2)}) async-start(), calls=%async_computation.10 | async-start | bytes 1310720 | tf_op jit(solution)/shard_map/all_gather | solution.py:42
  503.2 215.3 %all-reduce.9.cloned.1.call-start = ((), (), s32[]{:S(2)}) async-start(), calls=%async_computation.11 | async-start | bytes 2097152 | tf_op jit(solution)/shard_map/psum | solution.py:9
  531.3 215.3 %reduce-scatter.9.cloned.1.call-start = ((), (), s32[]{:S(2)}) async-start(), calls=%async_computation.12 | async-start | bytes 1310720 | tf_op jit(solution)/shard_map/reduce_scatter | solution.py:36
  721.3 55.5 %all-gather.11.cloned.1.call-start = ((), (), s32[]{:S(2)}) async-start(), calls=%async_computation.13 | async-start | bytes 1310720 | tf_op jit(solution)/shard_map/all_gather | solution.py:42
  749.9 215.2 %all-reduce.11.cloned.1.call-start = ((), (), s32[]{:S(2)}) async-start(), calls=%async_computation.14 | async-start | bytes 2097152 | tf_op jit(solution)/shard_map/psum | solution.py:9
  777.9 225.0 %reduce-scatter.11.cloned.1.call-start = ((), (), s32[]{:S(2)}) async-start(), calls=%async_computation.15 | async-start | bytes 2621440 | tf_op jit(solution)/shard_map/reduce_scatter | solution.py:46
  970.0 32.9 %copy-start.2 = (f32[128,1024]{1,0:T(8,128)S(1)}, f32[128,1024]{1,0:T(8,128)}, u32[]{:S(2)}) copy-start(f32[128,1024]{1,0:T(8,128)} %param.3) | copy-start | bytes 1572868
  970.0 34.0 %copy-start.3 = (f32[128,512]{1,0:T(8,128)S(1)}, f32[128,512]{1,0:T(8,128)}, u32[]{:S(2)}) copy-start(f32[128,512]{1,0:T(8,128)} %fusion.6) | copy-start | bytes 786436
  970.0 34.0 %copy-start.4 = (f32[128,512]{1,0:T(8,128)S(1)}, f32[128,512]{1,0:T(8,128)}, u32[]{:S(2)}) copy-start(f32[128,512]{1,0:T(8,128)} %fusion.4) | copy-start | bytes 786436
  970.0 34.0 %copy-start.5 = (f32[128,512]{1,0:T(8,128)S(1)}, f32[128,512]{1,0:T(8,128)}, u32[]{:S(2)}) copy-start(f32[128,512]{1,0:T(8,128)} %fusion.2) | copy-start | bytes 786436
  970.0 34.0 %copy-start.6 = (f32[128,512]{1,0:T(8,128)S(1)}, f32[128,512]{1,0:T(8,128)}, u32[]{:S(2)}) copy-start(f32[128,512]{1,0:T(8,128)} %fusion.8) | copy-start | bytes 786436
  1004.2 0.8 copy-start.7
Sparse Core Ops, SparseCore 0:
  9.9 29.4 all-gather.4
  42.8 184.8 all-reduce.4
  231.8 22.6 reduce-scatter.4
  257.8 26.7 all-gather.6
  287.9 184.8 all-reduce.6
  477.2 22.6 reduce-scatter.6
  503.3 26.8 all-gather.8
  533.6 184.8 all-reduce.8
  721.4 25.1 reduce-scatter.8
  750.0 26.7 all-gather.10
  780.3 184.8 all-reduce.10
  970.2 32.6 reduce-scatter.10
where the time goes:
time: 1010 us
  waiting for transfers between devices  961 us (95%)
  matrix products  27.6 us (3%)
  between operations  13.7 us (1%)
    psum x4, waiting for transfers between devices, spread(): return lax.psum(block, axis)  747 us
    all_gather x4, waiting for transfers between devices, per_device(): gathered = lax.all_gather(solved_part, 'pcol', axis=0, tiled=True)  110 us
    reduce_scatter x3, waiting for transfers between devices, per_device(): lax.psum_scatter(contract(panel_own, top_block), 'pcol', scatter_dimensio...  70.7 us
    reduce_scatter x1, waiting for transfers between devices, per_device(): lax.psum_scatter(contract(panel_own, factor), 'pcol', scatter_dimension=0...  32.8 us
    dot_general x8, matrix products, contract(): lax.dot_general(left, right, (((1,), (1,)), ((), ())), precision=lax.Prec...  27.6 us
  transfers between devices with their start and end apart: 12, of which 12 were waited for; matrix products, arithmetic and copies ran while one was open for 0% of the time, Pallas kernels for 0%

commit v1 on v0

--- a/solution.py
+++ b/solution.py
@@ -2,6 +2,7 @@
 import jax.numpy as jnp
 from jax import lax
 from jax.sharding import PartitionSpec as P
+from jax.lax import axis_index, axis_size, ppermute
 
 
 def spread(block, axis, source):
@@ -39,7 +40,29 @@
         block_inverse = inverses[section * block : (section + 1) * block]
         solved_part = contract(current, block_inverse)
         solved_head = jnp.where(row_at == section, solved_part, solved_head)
-        gathered = lax.all_gather(solved_part, "pcol", axis=0, tiled=True)
+
+        def _work_ticks(chunk):
+            blocks_here = []
+            n_shards = axis_size("pcol")
+            for k in [*range(n_shards)]:
+                blocks_here.append((k, (k + 1) % n_shards))
+            buffer = []
+            for k in [*range(n_shards)]:
+                buffer.append((k, (k - 1) % n_shards))
+            x_new, a_now = ([chunk], [chunk])
+            for _ in range(n_shards // 2):
+                even = ppermute(x_new[-1], "pcol", blocks_here)
+                x_new.append(even)
+            for _ in tuple(range((n_shards - 1) // 2)):
+                all_rows = ppermute(a_now[-1], "pcol", buffer)
+                a_now.append(all_rows)
+            near = jnp.concatenate([*x_new[::-1], *a_now[1:]], axis=0)
+            r_now = jnp.roll(
+                near, shift=(axis_index("pcol") - n_shards // 2) * chunk.shape[0], axis=0
+            )
+            return r_now
+
+        gathered = _work_ticks(solved_part)
         panel_full = spread(gathered, "prow", section)
         panel_own = jnp.where(col_at == section, panel_full, panel_own)
         own_panels.append(lax.dynamic_slice_in_dim(panel_full, col_at * rhs_width, rhs_width, 0))

time: 1010 us -> 962 us (0.952)
  waiting for transfers between devices: 961 us -> 893 us
  starting transfers between devices: 0.64 us -> 14.1 us
    all_gather x4 -> x0, waiting for transfers between devices: 110 us -> none  [per_device(): gathered = lax.all_gather(solved_part, 'pcol', axis=0, tiled=True)]
    ppermute x0 -> x12, waiting for transfers between devices: none -> 42.5 us  [the longest x8 42.5 us: _work_ticks(): even = ppermute(x_new[-1], 'pcol', blocks_here)]
    ppermute x0 -> x12, starting transfers between devices: none -> 13.6 us  [the longest x4 9.54 us: _work_ticks(): all_rows = ppermute(a_now[-1], 'pcol', buffer)]
  transfers between devices with their start and end apart: 12 -> 20, of which waited for: 12 -> 16; matrix products, arithmetic and copies ran while one was open for 0% -> 0% of each run, Pallas kernels for 0% -> 0%
where the time goes in v1:
time: 962 us
  waiting for transfers between devices  893 us (93%)
  matrix products  26.3 us (3%)
  other arithmetic  14.4 us (1%)
  starting transfers between devices  14.1 us (1%)
  between operations  13.6 us (1%)
    psum x4, waiting for transfers between devices, spread(): return lax.psum(block, axis)  746 us
    reduce_scatter x3, waiting for transfers between devices, per_device(): lax.psum_scatter(contract(panel_own, top_block), 'pcol', scatter_dimensio...  70.8 us
    ppermute x8, waiting for transfers between devices, _work_ticks(): even = ppermute(x_new[-1], 'pcol', blocks_here)  42.5 us
    reduce_scatter x1, waiting for transfers between devices, per_device(): lax.psum_scatter(contract(panel_own, factor), 'pcol', scatter_dimension=0...  32.8 us
    dot_general x8, matrix products, contract(): lax.dot_general(left, right, (((1,), (1,)), ((), ())), precision=lax.Prec...  26.3 us
  transfers between devices with their start and end apart: 20, of which 16 were waited for; matrix products, arithmetic and copies ran while one was open for 0% of the time, Pallas kernels for 0%

profile of v1, /device:TPU:1, one launch (start us, length us, event | category | flops | bytes accessed | tf_op | source)
XLA Modules:
  0.0 961.7 jit_solution(14776746625828920673)
XLA Ops:
  6.5 2.6 fusion.40
  9.2 2.2 collective-permute-start
  11.4 1.5 collective-permute-start.2
  12.9 3.7 collective-permute-done
  16.6 1.8 collective-permute-start.1
  18.4 0.0 collective-permute-done.2
  18.4 5.4 collective-permute-done.1
  23.7 2.5 fusion.28
  26.3 0.0 all-reduce.5.cloned.1.call-update
  26.3 0.0 reduce-scatter.5.cloned.1.call-start
  26.4 0.0 copy-start.1
  26.4 188.4 %all-reduce.5.cloned.1.call-done = f32[512,512]{1,0:T(8,128)} async-done(((f32[512,512]{1,0:T(8,128)}), f32[512,512]{1,0:T(8,128)}) %all-reduce.5.cloned.1.call-update) | async-done | bytes 1048592 | tf_op jit(solution)/shard_map/psum | solution.py:10
  214.8 4.1 fusion.42
  218.9 0.0 reduce-scatter.5.cloned.1.call-update
  218.9 0.0 all-reduce.7.cloned.1.call-start
  219.0 22.7 %reduce-scatter.5.cloned.1.call-done = f32[128,512]{1,0:T(8,128)} async-done(((f32[512,512]{1,0:T(8,128)}), f32[128,512]{1,0:T(8,128)}) %reduce-scatter.5.cloned.1.call-update) | async-done | bytes 262160 | tf_op jit(solution)/shard_map/reduce_scatter | solution.py:37
  241.7 2.5 fusion.38
  244.2 0.1 collective-permute-start.3
  244.3 2.7 collective-permute-start.5
  246.9 4.2 collective-permute-done.3
  251.2 0.0 collective-permute-start.4
  251.2 0.0 collective-permute-done.5
  251.2 6.4 collective-permute-done.4
  257.6 2.5 fusion.20
  260.1 0.0 all-reduce.7.cloned.1.call-update
  260.2 0.2 reduce-scatter.7.cloned.1.call-start
  260.4 186.0 %all-reduce.7.cloned.1.call-done = f32[512,512]{1,0:T(8,128)} async-done(((f32[512,512]{1,0:T(8,128)}), f32[512,512]{1,0:T(8,128)}) %all-reduce.7.cloned.1.call-update) | async-done | bytes 1048592 | tf_op jit(solution)/shard_map/psum | solution.py:10
  446.4 1.4 select_select_fusion
  447.8 2.8 fusion.46
  450.7 0.0 reduce-scatter.7.cloned.1.call-update
  450.7 0.0 all-reduce.9.cloned.1.call-start
  450.7 22.8 %reduce-scatter.7.cloned.1.call-done = f32[128,512]{1,0:T(8,128)} async-done(((f32[512,512]{1,0:T(8,128)}), f32[128,512]{1,0:T(8,128)}) %reduce-scatter.7.cloned.1.call-update) | async-done | bytes 262160 | tf_op jit(solution)/shard_map/reduce_scatter | solution.py:37
  473.5 3.3 fusion.36
  476.8 0.0 collective-permute-start.6
  476.8 2.7 collective-permute-start.8
  479.4 4.6 collective-permute-done.6
  484.1 0.0 collective-permute-start.7
  484.1 0.0 collective-permute-done.8
  484.1 6.7 collective-permute-done.7
  490.8 3.3 fusion.12
  494.1 0.0 all-reduce.9.cloned.1.call-update
  494.1 0.0 reduce-scatter.9.cloned.1.call-start
  494.2 186.0 %all-reduce.9.cloned.1.call-done = f32[512,512]{1,0:T(8,128)} async-done(((f32[512,512]{1,0:T(8,128)}), f32[512,512]{1,0:T(8,128)}) %all-reduce.9.cloned.1.call-update) | async-done | bytes 1048592 | tf_op jit(solution)/shard_map/psum | solution.py:10
  680.2 2.8 fusion.44
  683.0 0.0 reduce-scatter.9.cloned.1.call-update
  683.1 0.0 all-reduce.11.cloned.1.call-start
  683.1 25.3 %reduce-scatter.9.cloned.1.call-done = f32[128,512]{1,0:T(8,128)} async-done(((f32[512,512]{1,0:T(8,128)}), f32[128,512]{1,0:T(8,128)}) %reduce-scatter.9.cloned.1.call-update) | async-done | bytes 262160 | tf_op jit(solution)/shard_map/reduce_scatter | solution.py:37
  708.4 3.3 fusion.34
  711.6 0.0 collective-permute-start.9
  711.6 2.7 collective-permute-start.11
  714.3 4.7 collective-permute-done.9
  719.0 0.0 collective-permute-start.10
  719.0 6.7 collective-permute-done.10
  725.8 3.3 fusion.4
  729.0 0.0 all-reduce.11.cloned.1.call-update
  729.1 0.0 reduce-scatter.11.cloned.1.call-start
  729.1 185.9 %all-reduce.11.cloned.1.call-done = f32[512,512]{1,0:T(8,128)} async-done(((f32[512,512]{1,0:T(8,128)}), f32[512,512]{1,0:T(8,128)}) %all-reduce.11.cloned.1.call-update) | async-done | bytes 1048592 | tf_op jit(solution)/shard_map/psum | solution.py:10
  915.0 4.9 fusion.32
  919.9 0.0 reduce-scatter.11.cloned.1.call-update
  919.9 32.8 %reduce-scatter.11.cloned.1.call-done = f32[128,1024]{1,0:T(8,128)} async-done(((f32[512,1024]{1,0:T(8,128)}), f32[128,1024]{1,0:T(8,128)}) %reduce-scatter.11.cloned.1.call-update) | async-done | bytes 524304 | tf_op jit(solution)/shard_map/reduce_scatter | solution.py:69
  952.8 1.1 sub.25
  953.9 0.2 slice_select_fusion
  954.1 0.0 copy-start.5
  954.1 0.8 copy-done.5
  (12 shorter events, 0.0 us)
Async XLA Ops:
  6.5 208.3 %copy-start = (f32[1024,512]{1,0:T(8,128)S(1)}, f32[1024,512]{1,0:T(8,128)}, u32[]{:S(2)}) copy-start(f32[1024,512]{1,0:T(8,128)} %param.6) | copy-start | bytes 6291460
  6.5 208.3 %all-reduce.5.cloned.1.call-start = ((), (), s32[]{:S(2)}) async-start(), calls=%async_computation.4 | async-start | bytes 2097152 | tf_op jit(solution)/shard_map/psum | solution.py:10
  9.2 17.2 %copy-start.3 = (f32[128,512]{1,0:T(8,128)}, f32[128,512]{1,0:T(8,128)S(1)}, u32[]{:S(2)}) copy-start(f32[128,512]{1,0:T(8,128)S(1)} %fusion.40) | copy-start | bytes 786436
  9.2 7.4 collective-permute-start
  11.4 7.0 collective-permute-start.2
  16.6 7.2 collective-permute-start.1
  26.3 215.4 %reduce-scatter.5.cloned.1.call-start = ((), (), s32[]{:S(2)}) async-start(), calls=%async_computation.5 | async-start | bytes 1310720 | tf_op jit(solution)/shard_map/reduce_scatter | solution.py:37
  26.4 215.3 %copy-start.1 = (f32[128,1024]{1,0:T(8,128)S(1)}, f32[128,1024]{1,0:T(8,128)}, u32[]{:S(2)}) copy-start(f32[128,1024]{1,0:T(8,128)} %param.5) | copy-start | bytes 1572868
  218.9 227.5 %all-reduce.7.cloned.1.call-start = ((), (), s32[]{:S(2)}) async-start(), calls=%async_computation.6 | async-start | bytes 2097152 | tf_op jit(solution)/shard_map/psum | solution.py:10
  244.2 7.0 collective-permute-start.3
  244.3 6.9 collective-permute-start.5
  251.2 6.4 collective-permute-start.4
  260.2 213.3 %reduce-scatter.7.cloned.1.call-start = ((), (), s32[]{:S(2)}) async-start(), calls=%async_computation.7 | async-start | bytes 1310720 | tf_op jit(solution)/shard_map/reduce_scatter | solution.py:37
  450.7 229.5 %all-reduce.9.cloned.1.call-start = ((), (), s32[]{:S(2)}) async-start(), calls=%async_computation.8 | async-start | bytes 2097152 | tf_op jit(solution)/shard_map/psum | solution.py:10
  476.8 7.3 collective-permute-start.6
  476.8 7.3 collective-permute-start.8
  484.1 6.7 collective-permute-start.7
  494.1 214.2 %reduce-scatter.9.cloned.1.call-start = ((), (), s32[]{:S(2)}) async-start(), calls=%async_computation.9 | async-start | bytes 1310720 | tf_op jit(solution)/shard_map/reduce_scatter | solution.py:37
  683.1 231.9 %all-reduce.11.cloned.1.call-start = ((), (), s32[]{:S(2)}) async-start(), calls=%async_computation.10 | async-start | bytes 2097152 | tf_op jit(solution)/shard_map/psum | solution.py:10
  711.6 7.4 collective-permute-start.9
  711.6 7.4 collective-permute-start.11
  719.0 6.7 collective-permute-start.10
  729.1 223.7 %reduce-scatter.11.cloned.1.call-start = ((), (), s32[]{:S(2)}) async-start(), calls=%async_computation.11 | async-start | bytes 2621440 | tf_op jit(solution)/shard_map/reduce_scatter | solution.py:69
  919.9 32.9 %copy-start.2 = (f32[128,1024]{1,0:T(8,128)S(1)}, f32[128,1024]{1,0:T(8,128)}, u32[]{:S(2)}) copy-start(f32[128,1024]{1,0:T(8,128)} %param.5) | copy-start | bytes 1572868
  919.9 34.0 %copy-start.4 = (f32[128,512]{1,0:T(8,128)S(1)}, f32[128,512]{1,0:T(8,128)}, u32[]{:S(2)}) copy-start(f32[128,512]{1,0:T(8,128)} %copy-done.3) | copy-start | bytes 786436
  954.1 0.8 copy-start.5
Sparse Core Ops, SparseCore 0:
  26.4 188.3 all-reduce.4
  219.0 22.6 reduce-scatter.4
  260.3 186.0 all-reduce.6
  450.8 22.6 reduce-scatter.6
  494.3 185.9 all-reduce.8
  683.2 25.1 reduce-scatter.8
  729.2 185.7 all-reduce.10
  920.0 32.6 reduce-scatter.10
